TPU v7x, 32 devices: a whole 2x2x4 slice. The times are simulated.
32 devices in a mesh: dom: 4 (over y, x), grp: 8 (over z, core).
Axes of the slice: x: 2, y: 2, z: 4, core: 2. Of those that a mesh axis runs over, the one named last changes fastest.
Arguments:
- features: bfloat16 [40960, 128], P(('dom', 'grp')), may hold values from -6 to 6
- send_dom: int32 [32, 4, 32], P(('dom', 'grp')), may hold values from 0 to 1279
- send_grp: int32 [32, 8, 32], P(('dom', 'grp')), may hold values from 0 to 1279
- tile_vals: bfloat16 [1536, 128, 128], P(('dom', 'grp')), may hold values from 0.049804688 to 1
- tile_tgt: int32 [1536], P(('dom', 'grp')), may hold values from 0 to 9, as said below
- tile_src: int32 [1536], P(('dom', 'grp')), may hold values from 0 to 12, as said below
- tile_count: int32 [32], P(('dom', 'grp')), may hold values from 13 to 48, as said below
- w_self: bfloat16 [128, 256], replicated, may hold values from -0.5 to 0.5
- w_neigh: bfloat16 [128, 256], replicated, may hold values from -0.5 to 0.5
- cotangent: bfloat16 [40960, 256], P(('dom', 'grp'))
Outputs:
- output: bfloat16 [40960, 256], P(('dom', 'grp'))
- grad_features: bfloat16 [40960, 128], P(('dom', 'grp'))
- grad_self: float32 [128, 256], replicated
- grad_neigh: float32 [128, 256], replicated
Inputs may be any that keep to these rules, and one draw needn't show every extreme that they name: `tile_tgt`: in every partition, tile slot t for t < 10 has target block t; other slots name any target block. `tile_src`: in every partition, tile slot t for t < 13 has source block t; other slots name any source block. `tile_count`: some partition has all 48 slots live in every draw.
All inputs are finite; a program needn't handle non-finite values.
Results may differ from a plain program's by a relative error of at most 0.0049.
Values may be sent and summed in bfloat16 or wider, within the bound.
No kernel may reach another device: no remote copies, remote signals or barrier semaphores. Data moves between devices by JAX's collectives and lax.ppermute only.
A program may use at most 64 MiB of HBM per device.

v0:
```python
import jax
import jax.numpy as jnp
from jax import lax
from jax.sharding import PartitionSpec as P


def per_device(
    features,
    send_dom,
    send_grp,
    tile_vals,
    tile_tgt,
    tile_src,
    tile_count,
    w_self,
    w_neigh,
    cotangent,
):
    tile_size = tile_vals.shape[1]
    width = features.shape[1]
    node_count = features.shape[0]
    block_count = node_count // tile_size
    dom_index = send_dom[0]
    grp_index = send_grp[0]
    dom_peers = dom_index.shape[0]
    recv_dom = lax.all_to_all(features[dom_index], "dom", split_axis=0, concat_axis=0, tiled=True)
    recv_grp = lax.all_to_all(features[grp_index], "grp", split_axis=0, concat_axis=0, tiled=True)
    source = jnp.concatenate(
        [features, recv_dom.reshape(-1, width), recv_grp.reshape(-1, width)], axis=0
    )
    source = source.reshape(-1, tile_size, width)
    source_count = source.shape[0]
    slot_count = tile_vals.shape[0]
    usable = jnp.arange(slot_count, dtype=jnp.int32) < tile_count[0]
    to_target = (
        (tile_tgt[None, :] == jnp.arange(block_count, dtype=jnp.int32)[:, None]) & usable[None, :]
    ).astype(jnp.float32)
    to_source = (
        (tile_src[None, :] == jnp.arange(source_count, dtype=jnp.int32)[:, None]) & usable[None, :]
    ).astype(jnp.float32)
    products = jnp.einsum(
        "tij,tjf->tif", tile_vals, source[tile_src], preferred_element_type=jnp.float32
    )
    summed = jnp.einsum("bt,tif->bif", to_target, products, precision=lax.Precision.HIGHEST)
    unit_column = jnp.ones((tile_size,), jnp.bfloat16)
    row_sums = jnp.einsum("tij,j->ti", tile_vals, unit_column, preferred_element_type=jnp.float32)
    degree = jnp.dot(to_target, row_sums, precision=lax.Precision.HIGHEST)
    agg = (summed / degree[:, :, None]).reshape(node_count, width).astype(jnp.bfloat16)
    preact = jnp.dot(features, w_self, preferred_element_type=jnp.float32) + jnp.dot(
        agg, w_neigh, preferred_element_type=jnp.float32
    )
    sigm = jax.nn.sigmoid(preact)
    output = (preact * sigm).astype(jnp.bfloat16)
    grad_pre = (cotangent.astype(jnp.float32) * sigm * (1.0 + preact * (1.0 - sigm))).astype(
        jnp.bfloat16
    )
    part_self = jnp.einsum("nf,nh->fh", features, grad_pre, preferred_element_type=jnp.float32)
    part_neigh = jnp.einsum("nf,nh->fh", agg, grad_pre, preferred_element_type=jnp.float32)
    grad_own = jnp.einsum("nh,fh->nf", grad_pre, w_self, preferred_element_type=jnp.float32)
    grad_agg = jnp.einsum("nh,fh->nf", grad_pre, w_neigh, preferred_element_type=jnp.float32)
    grad_agg = (grad_agg / degree.reshape(-1)[:, None]).astype(jnp.bfloat16)
    picked = grad_agg.reshape(block_count, tile_size, width)[tile_tgt]
    backward = jnp.einsum("tij,tif->tjf", tile_vals, picked, preferred_element_type=jnp.float32)
    grad_source = jnp.einsum(
        "st,tjf->sjf", to_source, backward, precision=lax.Precision.HIGHEST
    ).reshape(-1, width)
    dom_rows = dom_peers * dom_index.shape[1]
    back_dom = (
        grad_source[node_count : node_count + dom_rows]
        .reshape(dom_index.shape[0], dom_index.shape[1], width)
        .astype(jnp.bfloat16)
    )
    back_grp = (
        grad_source[node_count + dom_rows :]
        .reshape(grp_index.shape[0], grp_index.shape[1], width)
        .astype(jnp.bfloat16)
    )
    ret_dom = lax.all_to_all(back_dom, "dom", split_axis=0, concat_axis=0, tiled=True)
    ret_grp = lax.all_to_all(back_grp, "grp", split_axis=0, concat_axis=0, tiled=True)
    grad_self, grad_neigh = lax.psum((part_self, part_neigh), ("dom", "grp"))
    grad_total = grad_own + grad_source[:node_count]
    grad_total = grad_total.at[dom_index.reshape(-1)].add(
        ret_dom.reshape(-1, width).astype(jnp.float32)
    )
    grad_total = grad_total.at[grp_index.reshape(-1)].add(
        ret_grp.reshape(-1, width).astype(jnp.float32)
    )
    return (output, grad_total.astype(jnp.bfloat16), grad_self, grad_neigh)


def solution(mesh):
    return jax.shard_map(
        per_device,
        mesh=mesh,
        in_specs=(
            P(("dom", "grp"), None),
            P(("dom", "grp"), None, None),
            P(("dom", "grp"), None, None),
            P(("dom", "grp"), None, None),
            P(("dom", "grp")),
            P(("dom", "grp")),
            P(("dom", "grp")),
            P(),
            P(),
            P(("dom", "grp"), None),
        ),
        out_specs=(P(("dom", "grp"), None), P(("dom", "grp"), None), P(), P()),
        check_vma=False,
    )
```

profile of v0, /device:TPU:0, one launch (start us, length us, event | category | flops | bytes accessed | tf_op | source)
XLA Modules:
  0.0 210.0 jit_solution(4787525386066854471)
XLA Ops:
  7.2 0.0 copy-start
  7.2 0.8 compare_select_fusion.2
  8.0 0.1 reshape.166
  8.1 2.3 %gather_fusion = bf16[128,128]{1,0:T(8,128)(2,1)} fusion(bf16[1280,128]{1,0:T(8,128)(2,1)} %param.10, s32[1024]{0:T(1024)S(1)} %pad_clamp_fusion.3), kind=kCustom, calls=%fused_computation | custom fusion | bytes 66048 | tf_op jit(solution)/shard_map/gather | solution.py:26
  10.4 5.2 %all-to-all-start = ((bf16[4,32,128]{2,1,0:T(8,128)(2,1)}), bf16[4,32,128]{2,1,0:T(8,128)(2,1)S(1)}, u32[]{:S(2)}, u32[]{:S(2)}) async-start(bf16[4,32,128]{2,1,0:T(8,128)(2,1)} %bitcast.3), calls=%async_computation | async-start | bytes 65536 | tf_op jit(solution)/shard_map/all_to_all | solution.py:26
  15.6 0.8 reshape_squeeze.6
  16.3 0.8 reshape_squeeze.7
  17.1 0.7 compare_select_fusion
  18.4 0.7 compare_select_fusion.5
  19.1 0.7 compare_select_fusion.4
  19.8 0.1 reshape.174
  19.9 0.5 fusion.30
  20.4 1.4 fusion.34
  21.8 0.1 fusion.16
  21.9 1.5 gather_fusion.1
  23.4 4.9 %all-to-all-start.1 = ((bf16[8,32,128]{2,1,0:T(8,128)(2,1)}), bf16[8,32,128]{2,1,0:T(8,128)(2,1)S(1)}, u32[]{:S(2)}, u32[]{:S(2)}) async-start(bf16[8,32,128]{2,1,0:T(8,128)(2,1)} %bitcast.6), calls=%async_computation.1 | async-start | bytes 131072 | tf_op jit(solution)/shard_map/all_to_all | solution.py:27
  28.3 0.1 copy.17
  28.4 5.8 %all-to-all-done.1 = bf16[8,32,128]{2,1,0:T(8,128)(2,1)S(1)} async-done(((bf16[8,32,128]{2,1,0:T(8,128)(2,1)}), bf16[8,32,128]{2,1,0:T(8,128)(2,1)S(1)}, u32[]{:S(2)}, u32[]{:S(2)}) %all-to-all-start.1) | async-done | bytes 65568 | tf_op jit(solution)/shard_map/all_to_all | solution.py:27
  34.2 1.9 gather_fusion.2
  36.1 4.3 %fusion.35 = f32[48,128,128]{2,1,0:T(8,128)} fusion(bf16[48,128,128]{2,1,0:T(8,128)(2,1)} %gather_fusion.2, bf16[48,128,128]{2,1,0:T(8,128)(2,1)S(1)} %copy-done), kind=kOutput, calls=%fused_computation.55 | convolution fusion | flops 201326592 | bytes 6291456 | tf_op jit(solution)/shard_map/tij,tjf->tif/dot_general | solution.py:41
  40.4 3.6 %copy.22 = f32[48,128,128]{1,0,2:T(8,128)} copy(f32[48,128,128]{2,1,0:T(8,128)} %fusion.35) | data formatting | bytes 6291456 | tf_op jit(solution)/shard_map/tij,tjf->tif/dot_general | solution.py:41
  44.1 3.3 %fusion.8 = bf16[10,128,128]{2,0,1:T(8,128)(2,1)S(1)} fusion(f32[48,128,128]{1,0,2:T(8,128)} %copy.22, f32[10,128]{0,1:T(8,128)S(1)} %copy.17, s32[48]{0:T(128)S(1)} %copy-done.5, pred[48]{0:T(512)(128)(4,1)S(1)} %iota_compare_fusion.2), kind=kOutput, calls=%fused_computation.18 | convolution fusion | flops 94700480 | bytes 3478768 | tf_op jit(solution)/shard_map/bt,tif->bif/dot_general | solution.py:44
  47.3 0.1 copy.18
  47.5 1.6 multiply_convert_fusion
  49.1 1.0 fusion.37
  50.0 0.3 fusion.4
  50.4 1.9 gather_fusion.3
  52.3 3.7 %fusion.36 = f32[48,128,128]{2,1,0:T(8,128)} fusion(bf16[48,128,128]{2,1,0:T(8,128)(2,1)} %gather_fusion.3, bf16[48,128,128]{2,1,0:T(8,128)(2,1)S(1)} %copy-done), kind=kOutput, calls=%fused_computation.56 | convolution fusion | flops 201326592 | bytes 6291456 | tf_op jit(solution)/shard_map/tij,tif->tjf/dot_general | solution.py:63
  56.1 3.6 %copy.24 = f32[48,128,128]{1,0,2:T(8,128)} copy(f32[48,128,128]{2,1,0:T(8,128)} %fusion.36) | data formatting | bytes 6291456 | tf_op jit(solution)/shard_map/tij,tif->tjf/dot_general | solution.py:63
  59.7 4.0 %fusion.33 = (bf16[13,128,128]{2,0,1:T(8,128)(2,1)S(1)}, f32[13,128,128]{2,0,1:T(8,128)}) fusion(f32[48,128,128]{1,0,2:T(8,128)} %copy.24, s32[48]{0:T(128)S(1)} %copy-done.6, pred[48]{0:T(512)(128)(4,1)S(1)} %iota_compare_fusion.2), kind=kOutput, calls=%fused_computation.53 | convolution fusion | flops 122897632 | bytes 4423920 | tf_op jit(solution)/shard_map/st,tjf->sjf/dot_general | solution.py:64
  63.7 0.1 slice.29
  63.8 0.6 copy.25
  64.4 4.2 %all-to-all-start.2 = ((bf16[4,32,128]{2,1,0:T(8,128)(2,1)}), bf16[4,32,128]{2,1,0:T(8,128)(2,1)S(1)}, u32[]{:S(2)}, u32[]{:S(2)}) async-start(bf16[4,32,128]{2,1,0:T(8,128)(2,1)} %bitcast.26), calls=%async_computation.2 | async-start | bytes 65536 | tf_op jit(solution)/shard_map/all_to_all | solution.py:78
  68.6 1.0 convolution_bitcast_fusion
  69.7 0.1 slice.30
  69.7 1.4 copy.19
  71.2 0.6 copy.20
  71.8 0.0 all-reduce.3.cloned.1.call-update
  71.8 1.5 all-to-all-done.2
  73.4 3.4 %all-to-all-start.3 = ((bf16[8,32,128]{2,1,0:T(8,128)(2,1)}), bf16[8,32,128]{2,1,0:T(8,128)(2,1)S(1)}, u32[]{:S(2)}, u32[]{:S(2)}) async-start(bf16[8,32,128]{2,1,0:T(8,128)(2,1)} %bitcast.21), calls=%async_computation.3 | async-start | bytes 131072 | tf_op jit(solution)/shard_map/all_to_all | solution.py:79
  76.8 1.2 convolution_add_fusion.1
  77.9 3.1 %scatter_custom_fusion = f32[1280,128]{1,0:T(8,128)} fusion(f32[1280,128]{1,0:T(8,128)} %convolution_add_fusion.1, s32[128]{0:T(128)S(1)} %fusion.29, bf16[128,128]{1,0:T(8,128)(2,1)S(1)} %bitcast.80), kind=kCustom, calls=%fused_computation.23 | custom fusion | flops 32768 | bytes 688128 | tf_op jit(solution)/shard_map/scatter-add | solution.py:82
  81.0 1.6 all-to-all-done.3
  82.6 3.7 %scatter_custom_fusion.1 = f32[1280,128]{1,0:T(8,128)} fusion(f32[1280,128]{1,0:T(8,128)} %scatter_custom_fusion, s32[256]{0:T(256)S(1)} %bitcast.83, bf16[256,128]{1,0:T(8,128)(2,1)S(1)} %bitcast.77), kind=kCustom, calls=%fused_computation.21 | custom fusion | flops 65536 | bytes 720896 | tf_op jit(solution)/shard_map/scatter-add | solution.py:85
  86.3 1.8 convert_element_type.55
  88.1 111.7 %all-reduce.3.cloned.1.call-done = (f32[128,256]{0,1:T(8,128)}, f32[128,256]{1,0:T(8,128)}) async-done(((f32[128,256]{0,1:T(8,128)}, f32[128,256]{1,0:T(8,128)}), (f32[128,256]{0,1:T(8,128)}, f32[128,256]{1,0:T(8,128)})) %all-reduce.3.cloned.1.call-update) | async-done | bytes 262160 | tf_op jit(solution)/shard_map/psum | solution.py:80
  199.9 1.7 copy.21
  201.5 1.6 copy.31
  (27 shorter events, 0.1 us)
Async XLA Ops:
  7.2 12.7 %copy-start = (bf16[48,128,128]{2,1,0:T(8,128)(2,1)S(1)}, bf16[48,128,128]{2,1,0:T(8,128)(2,1)}, u32[]{:S(2)}) copy-start(bf16[48,128,128]{2,1,0:T(8,128)(2,1)} %param.13) | copy-start | bytes 4718596
  7.2 13.2 %copy-start.1 = (bf16[1280,128]{1,0:T(8,128)(2,1)S(1)}, bf16[1280,128]{1,0:T(8,128)(2,1)}, u32[]{:S(2)}) copy-start(bf16[1280,128]{1,0:T(8,128)(2,1)} %param.10) | copy-start | bytes 983044
  7.2 13.2 %copy-start.3 = (bf16[128,256]{1,0:T(8,128)(2,1)S(1)}, bf16[128,256]{1,0:T(8,128)(2,1)}, u32[]{:S(2)}) copy-start(bf16[128,256]{1,0:T(8,128)(2,1)} %param.17) | copy-start | bytes 196612
  10.4 13.0 %all-to-all-start = ((bf16[4,32,128]{2,1,0:T(8,128)(2,1)}), bf16[4,32,128]{2,1,0:T(8,128)(2,1)S(1)}, u32[]{:S(2)}, u32[]{:S(2)}) async-start(bf16[4,32,128]{2,1,0:T(8,128)(2,1)} %bitcast.3), calls=%async_computation | async-start | bytes 65536 | tf_op jit(solution)/shard_map/all_to_all | solution.py:26
  19.8 1.9 copy-start.5
  23.4 10.8 %all-to-all-start.1 = ((bf16[8,32,128]{2,1,0:T(8,128)(2,1)}), bf16[8,32,128]{2,1,0:T(8,128)(2,1)S(1)}, u32[]{:S(2)}, u32[]{:S(2)}) async-start(bf16[8,32,128]{2,1,0:T(8,128)(2,1)} %bitcast.6), calls=%async_computation.1 | async-start | bytes 131072 | tf_op jit(solution)/shard_map/all_to_all | solution.py:27
  44.1 3.4 %copy-start.2 = (f32[1280,256]{1,0:T(8,128)S(1)}, f32[1280,256]{1,0:T(8,128)}, u32[]{:S(2)}) copy-start(f32[1280,256]{1,0:T(8,128)} %fusion.34) | copy-start | bytes 3932164
  44.1 3.4 %copy-start.7 = (bf16[1280,256]{1,0:T(8,128)(2,1)S(1)}, bf16[1280,256]{1,0:T(8,128)(2,1)}, u32[]{:S(2)}) copy-start(bf16[1280,256]{1,0:T(8,128)(2,1)} %param.19) | copy-start | bytes 1966084
  44.1 3.4 %copy-start.8 = (bf16[128,256]{1,0:T(8,128)(2,1)S(1)}, bf16[128,256]{1,0:T(8,128)(2,1)}, u32[]{:S(2)}) copy-start(bf16[128,256]{1,0:T(8,128)(2,1)} %param.18) | copy-start | bytes 196612
  56.1 3.6 %copy-start.6 = (s32[48]{0:T(128)S(1)}, s32[48]{0:T(128)}, u32[]{:S(2)}) copy-start(s32[48]{0:T(128)} %param.15) | copy-start | bytes 580
  64.4 9.0 %all-to-all-start.2 = ((bf16[4,32,128]{2,1,0:T(8,128)(2,1)}), bf16[4,32,128]{2,1,0:T(8,128)(2,1)S(1)}, u32[]{:S(2)}, u32[]{:S(2)}) async-start(bf16[4,32,128]{2,1,0:T(8,128)(2,1)} %bitcast.26), calls=%async_computation.2 | async-start | bytes 65536 | tf_op jit(solution)/shard_map/all_to_all | solution.py:78
  68.6 8.1 %copy-start.4 = (bf16[128,256]{1,0:T(8,128)(2,1)S(1)}, bf16[128,256]{1,0:T(8,128)(2,1)}, u32[]{:S(2)}) copy-start(bf16[128,256]{1,0:T(8,128)(2,1)} %param.17) | copy-start | bytes 196612
  68.6 131.3 %all-reduce.3.cloned.1.call-start = ((), (), s32[]{:S(2)}) async-start(), calls=%async_computation.4 | async-start | bytes 524288 | tf_op jit(solution)/shard_map/psum | solution.py:80
  73.4 9.2 %all-to-all-start.3 = ((bf16[8,32,128]{2,1,0:T(8,128)(2,1)}), bf16[8,32,128]{2,1,0:T(8,128)(2,1)S(1)}, u32[]{:S(2)}, u32[]{:S(2)}) async-start(bf16[8,32,128]{2,1,0:T(8,128)(2,1)} %bitcast.21), calls=%async_computation.3 | async-start | bytes 131072 | tf_op jit(solution)/shard_map/all_to_all | solution.py:79
Sparse Core Ops, SparseCore 0:
  75.7 124.1 all-reduce.2
where the time goes:
time: 211 us; the launch traced here: 210 us
  waiting for transfers between devices  121 us (57%)
  local copies, waits for them, and re-layouts  22.9 us (11%)
  matrix products  22.5 us (11%)
  starting transfers between devices  17.6 us (8%)
  between operations  14.8 us (7%)
  other arithmetic  11.5 us (5%)
    psum x1, waiting for transfers between devices, per_device(): grad_self, grad_neigh = lax.psum((part_self, part_neigh), ('dom', 'grp'))  112 us
    all_to_all x1, waiting for transfers between devices, per_device(): lax.all_to_all(features[grp_index], 'grp', split_axis=0, concat_axis=0, t...  5.79 us
    all_to_all x1, starting transfers between devices, per_device(): lax.all_to_all(features[dom_index], 'dom', split_axis=0, concat_axis=0, t...  5.16 us
    all_to_all x1, starting transfers between devices, per_device(): lax.all_to_all(features[grp_index], 'grp', split_axis=0, concat_axis=0, t...  4.88 us
    dot_general x1, matrix products, per_device(): jnp.einsum('tij,tjf->tif', tile_vals, source[tile_src], preferred_element...  4.3 us
  transfers between devices with their start and end apart: 5, of which 4 were waited for; matrix products, arithmetic and copies ran while one was open for 10% of the time, Pallas kernels for 0%

commit v1 on v0

--- a/solution.py
+++ b/solution.py
@@ -2,6 +2,22 @@
 import jax.numpy as jnp
 from jax import lax
 from jax.sharding import PartitionSpec as P
+
+
+def exchange_in_pairs(x, axis, split, join):
+    ways, here = (lax.axis_size(axis), lax.axis_index(axis))
+    width = x.shape[split] // ways
+    shape = list(x.shape)
+    shape[split] = width
+    height = shape[join]
+    shape[join] = height * ways
+    full = jnp.zeros(shape, x.dtype)
+    for mask in range(ways):
+        part = lax.dynamic_slice_in_dim(x, (here ^ mask) * width, width, axis=split)
+        if mask:
+            part = lax.ppermute(part, axis, [(d, d ^ mask) for d in range(ways)])
+        full = lax.dynamic_update_slice_in_dim(full, part, (here ^ mask) * height, axis=join)
+    return full
 
 
 def per_device(
@@ -23,7 +39,7 @@
     dom_index = send_dom[0]
     grp_index = send_grp[0]
     dom_peers = dom_index.shape[0]
-    recv_dom = lax.all_to_all(features[dom_index], "dom", split_axis=0, concat_axis=0, tiled=True)
+    recv_dom = exchange_in_pairs(features[dom_index], "dom", 0, 0)
     recv_grp = lax.all_to_all(features[grp_index], "grp", split_axis=0, concat_axis=0, tiled=True)
     source = jnp.concatenate(
         [features, recv_dom.reshape(-1, width), recv_grp.reshape(-1, width)], axis=0

time: 211 us -> 207 us (0.981)
  other arithmetic: 11.5 us -> 7.23 us
    all_to_all x1 -> x0, starting transfers between devices: 5.16 us -> none  [per_device(): lax.all_to_all(features[dom_index], 'dom', split_axis=0, concat_axis=0, t...]
    all_to_all x1, waiting for transfers between devices: 5.79 us -> 0.78 us  [per_device(): lax.all_to_all(features[grp_index], 'grp', split_axis=0, concat_axis=0, t...]
    ppermute x0 -> x3, starting transfers between devices: none -> 4.54 us  [exchange_in_pairs(): part = lax.ppermute(part, axis, [(d, d ^ mask) for d in range(ways)])]
    psum x1, waiting for transfers between devices: 112 us -> 115 us  [per_device(): grad_self, grad_neigh = lax.psum((part_self, part_neigh), ('dom', 'grp'))]
  transfers between devices with their start and end apart: 5 -> 7, of which waited for: 4 -> 4; matrix products, arithmetic and copies ran while one was open for 10% -> 8% of each run, Pallas kernels for 0% -> 0%
where the time goes in v1:
time: 207 us; the launch traced here: 206 us
  waiting for transfers between devices  121 us (58%)
  local copies, waits for them, and re-layouts  23.2 us (11%)
  matrix products  22.5 us (11%)
  starting transfers between devices  17.9 us (9%)
  between operations  14.9 us (7%)
  other arithmetic  7.23 us (3%)
    psum x1, waiting for transfers between devices, per_device(): grad_self, grad_neigh = lax.psum((part_self, part_neigh), ('dom', 'grp'))  115 us
    all_to_all x1, starting transfers between devices, per_device(): lax.all_to_all(features[grp_index], 'grp', split_axis=0, concat_axis=0, t...  5.33 us
    ppermute x3, starting transfers between devices, exchange_in_pairs(): part = lax.ppermute(part, axis, [(d, d ^ mask) for d in range(ways)])  4.54 us
    all_to_all x1, starting transfers between devices, per_device(): lax.all_to_all(back_grp, 'grp', split_axis=0, concat_axis=0, tiled=True)  4.33 us
    dot_general x1, matrix products, per_device(): jnp.einsum('tij,tjf->tif', tile_vals, source[tile_src], preferred_element...  4.3 us
  transfers between devices with their start and end apart: 7, of which 4 were waited for; matrix products, arithmetic and copies ran while one was open for 8% of the time, Pallas kernels for 0%

profile of v1, /device:TPU:0, one launch (start us, length us, event | category | flops | bytes accessed | tf_op | source)
XLA Modules:
  0.0 206.3 jit_solution(2229529775570928119)
XLA Ops:
  7.2 0.8 compare_select_fusion.2
  8.0 0.1 reshape.166
  8.1 1.7 gather_fusion
  9.8 3.0 %collective-permute-start = (bf16[1,32,128]{2,1,0:T(8,128)(2,1)S(1)}, bf16[1,32,128]{2,1,0:T(8,128)(2,1)S(1)}, u32[]{:S(2)}, u32[]{:S(2)}) collective-permute-start(bf16[1,32,128]{2,1,0:T(8,128)(2,1)S(1)} %get-tuple-element.18), channel_id=1, source_target_pairs={{0,8},{8,0},{16,24},{24,16},{1,9},{9,1},{17,25},{25,17},{2,10},{10... | collective-permute-start | bytes 24584 | tf_op jit(solution)/shard_map/ppermute | solution.py:18
  12.8 1.5 collective-permute-start.1
  14.4 0.0 collective-permute-start.2
  14.4 0.7 compare_select_fusion
  15.1 0.1 reshape.174
  15.2 2.4 %gather_fusion.1 = bf16[256,128]{1,0:T(8,128)(2,1)} fusion(bf16[1280,128]{1,0:T(8,128)(2,1)} %param.10, s32[1024]{0:T(1024)S(1)} %pad_clamp_fusion.2), kind=kCustom, calls=%fused_computation.1 | custom fusion | bytes 132096 | tf_op jit(solution)/shard_map/gather | solution.py:43
  17.5 5.3 %all-to-all-start = ((bf16[8,32,128]{2,1,0:T(8,128)(2,1)}), bf16[8,32,128]{2,1,0:T(8,128)(2,1)S(1)}, u32[]{:S(2)}, u32[]{:S(2)}) async-start(bf16[8,32,128]{2,1,0:T(8,128)(2,1)} %bitcast.6), calls=%async_computation | async-start | bytes 131072 | tf_op jit(solution)/shard_map/all_to_all | solution.py:43
  22.9 0.8 reshape_squeeze.6
  23.6 0.8 reshape_squeeze.7
  24.4 0.7 compare_select_fusion.5
  25.7 0.5 fusion.30
  26.2 1.4 fusion.34
  27.7 0.1 fusion.16
  27.8 0.1 copy.17
  28.0 0.8 all-to-all-done
  28.8 2.0 gather_fusion.2
  30.8 4.3 %fusion.35 = f32[48,128,128]{2,1,0:T(8,128)} fusion(bf16[48,128,128]{2,1,0:T(8,128)(2,1)} %gather_fusion.2, bf16[48,128,128]{2,1,0:T(8,128)(2,1)S(1)} %copy-done), kind=kOutput, calls=%fused_computation.62 | convolution fusion | flops 201326592 | bytes 6291456 | tf_op jit(solution)/shard_map/tij,tjf->tif/dot_general | solution.py:57
  35.1 3.6 %copy.22 = f32[48,128,128]{1,0,2:T(8,128)} copy(f32[48,128,128]{2,1,0:T(8,128)} %fusion.35) | data formatting | bytes 6291456 | tf_op jit(solution)/shard_map/tij,tjf->tif/dot_general | solution.py:57
  38.7 3.3 %fusion.8 = bf16[10,128,128]{2,0,1:T(8,128)(2,1)S(1)} fusion(f32[48,128,128]{1,0,2:T(8,128)} %copy.22, f32[10,128]{0,1:T(8,128)S(1)} %copy.17, s32[48]{0:T(128)S(1)} %copy-done.5, pred[48]{0:T(512)(128)(4,1)S(1)} %iota_compare_fusion.2), kind=kOutput, calls=%fused_computation.18 | convolution fusion | flops 94700480 | bytes 3478768 | tf_op jit(solution)/shard_map/bt,tif->bif/dot_general | solution.py:60
  41.9 0.1 copy.18
  42.1 1.7 multiply_convert_fusion
  43.7 1.0 fusion.37
  44.7 0.3 fusion.4
  45.0 2.0 gather_fusion.3
  47.0 3.7 %fusion.36 = f32[48,128,128]{2,1,0:T(8,128)} fusion(bf16[48,128,128]{2,1,0:T(8,128)(2,1)} %gather_fusion.3, bf16[48,128,128]{2,1,0:T(8,128)(2,1)S(1)} %copy-done), kind=kOutput, calls=%fused_computation.63 | convolution fusion | flops 201326592 | bytes 6291456 | tf_op jit(solution)/shard_map/tij,tif->tjf/dot_general | solution.py:79
  50.7 3.6 %copy.24 = f32[48,128,128]{1,0,2:T(8,128)} copy(f32[48,128,128]{2,1,0:T(8,128)} %fusion.36) | data formatting | bytes 6291456 | tf_op jit(solution)/shard_map/tij,tif->tjf/dot_general | solution.py:79
  54.3 4.0 %fusion.33 = (bf16[13,128,128]{2,0,1:T(8,128)(2,1)S(1)}, f32[13,128,128]{2,0,1:T(8,128)}) fusion(f32[48,128,128]{1,0,2:T(8,128)} %copy.24, s32[48]{0:T(128)S(1)} %copy-done.6, pred[48]{0:T(512)(128)(4,1)S(1)} %iota_compare_fusion.2), kind=kOutput, calls=%fused_computation.60 | convolution fusion | flops 122897632 | bytes 4423920 | tf_op jit(solution)/shard_map/st,tjf->sjf/dot_general | solution.py:80
  58.4 0.1 slice.29
  58.4 0.6 copy.25
  59.1 3.7 %all-to-all-start.1 = ((bf16[4,32,128]{2,1,0:T(8,128)(2,1)}), bf16[4,32,128]{2,1,0:T(8,128)(2,1)S(1)}, u32[]{:S(2)}, u32[]{:S(2)}) async-start(bf16[4,32,128]{2,1,0:T(8,128)(2,1)} %bitcast.26), calls=%async_computation.1 | async-start | bytes 65536 | tf_op jit(solution)/shard_map/all_to_all | solution.py:94
  62.8 1.0 convolution_bitcast_fusion
  63.8 0.1 slice.30
  63.9 1.4 copy.19
  65.3 0.6 copy.20
  65.9 0.0 all-reduce.3.cloned.1.call-update
  66.0 1.5 all-to-all-done.1
  67.5 4.3 %all-to-all-start.2 = ((bf16[8,32,128]{2,1,0:T(8,128)(2,1)}), bf16[8,32,128]{2,1,0:T(8,128)(2,1)}, u32[]{:S(2)}, u32[]{:S(2)}) async-start(bf16[8,32,128]{2,1,0:T(8,128)(2,1)} %bitcast.21), calls=%async_computation.2 | async-start | bytes 131072 | tf_op jit(solution)/shard_map/all_to_all | solution.py:95
  71.9 1.2 convolution_add_fusion.1
  73.0 1.7 scatter_custom_fusion
  74.8 3.1 %all-to-all-done.2 = bf16[8,32,128]{2,1,0:T(8,128)(2,1)} async-done(((bf16[8,32,128]{2,1,0:T(8,128)(2,1)}), bf16[8,32,128]{2,1,0:T(8,128)(2,1)}, u32[]{:S(2)}, u32[]{:S(2)}) %all-to-all-start.2) | async-done | bytes 65568 | tf_op jit(solution)/shard_map/all_to_all | solution.py:95
  77.9 2.5 %scatter_custom_fusion.1 = f32[1280,128]{1,0:T(8,128)S(1)} fusion(f32[1280,128]{1,0:T(8,128)S(1)} %scatter_custom_fusion, s32[256]{0:T(256)S(1)} %bitcast.83, bf16[256,128]{1,0:T(8,128)(2,1)} %bitcast.25), kind=kCustom, calls=%fused_computation.21 | custom fusion | flops 65536 | bytes 720896 | tf_op jit(solution)/shard_map/scatter-add | solution.py:101
  80.4 0.8 convert_element_type.55
  81.1 115.1 %all-reduce.3.cloned.1.call-done = (f32[128,256]{0,1:T(8,128)}, f32[128,256]{1,0:T(8,128)}) async-done(((f32[128,256]{0,1:T(8,128)}, f32[128,256]{1,0:T(8,128)}), (f32[128,256]{0,1:T(8,128)}, f32[128,256]{1,0:T(8,128)})) %all-reduce.3.cloned.1.call-update) | async-done | bytes 262160 | tf_op jit(solution)/shard_map/psum | solution.py:96
  196.2 1.7 copy.21
  197.9 1.6 copy.35
  (36 shorter events, 0.2 us)
Async XLA Ops:
  7.2 18.6 %copy-start = (bf16[48,128,128]{2,1,0:T(8,128)(2,1)S(1)}, bf16[48,128,128]{2,1,0:T(8,128)(2,1)}, u32[]{:S(2)}) copy-start(bf16[48,128,128]{2,1,0:T(8,128)(2,1)} %param.13) | copy-start | bytes 4718596
  7.2 19.1 %copy-start.1 = (bf16[1280,128]{1,0:T(8,128)(2,1)S(1)}, bf16[1280,128]{1,0:T(8,128)(2,1)}, u32[]{:S(2)}) copy-start(bf16[1280,128]{1,0:T(8,128)(2,1)} %param.10) | copy-start | bytes 983044
  7.2 19.1 %copy-start.3 = (bf16[128,256]{1,0:T(8,128)(2,1)S(1)}, bf16[128,256]{1,0:T(8,128)(2,1)}, u32[]{:S(2)}) copy-start(bf16[128,256]{1,0:T(8,128)(2,1)} %param.17) | copy-start | bytes 196612
  9.8 18.1 %collective-permute-start = (bf16[1,32,128]{2,1,0:T(8,128)(2,1)S(1)}, bf16[1,32,128]{2,1,0:T(8,128)(2,1)S(1)}, u32[]{:S(2)}, u32[]{:S(2)}) collective-permute-start(bf16[1,32,128]{2,1,0:T(8,128)(2,1)S(1)} %get-tuple-element.18), channel_id=1, source_target_pairs={{0,8},{8,0},{16,24},{24,16},{1,9},{9,1},{17,25},{25,17},{2,10},{10... | collective-permute-start | bytes 24584 | tf_op jit(solution)/shard_map/ppermute | solution.py:18
  12.8 15.1 %collective-permute-start.1 = (bf16[1,32,128]{2,1,0:T(8,128)(2,1)S(1)}, bf16[1,32,128]{2,1,0:T(8,128)(2,1)S(1)}, u32[]{:S(2)}, u32[]{:S(2)}) collective-permute-start(bf16[1,32,128]{2,1,0:T(8,128)(2,1)S(1)} %get-tuple-element.17), channel_id=1, source_target_pairs={{0,16},{8,24},{16,0},{24,8},{1,17},{9,25},{17,1},{25,9},{2,18},{10... | collective-permute-start | bytes 24584 | tf_op jit(solution)/shard_map/ppermute | solution.py:18
  14.4 13.6 %collective-permute-start.2 = (bf16[1,32,128]{2,1,0:T(8,128)(2,1)S(1)}, bf16[1,32,128]{2,1,0:T(8,128)(2,1)S(1)}, u32[]{:S(2)}, u32[]{:S(2)}) collective-permute-start(bf16[1,32,128]{2,1,0:T(8,128)(2,1)S(1)} %get-tuple-element.16), channel_id=1, source_target_pairs={{0,24},{8,16},{16,8},{24,0},{1,25},{9,17},{17,9},{25,1},{2,26},{10... | collective-permute-start | bytes 24584 | tf_op jit(solution)/shard_map/ppermute | solution.py:18
  17.5 11.2 %all-to-all-start = ((bf16[8,32,128]{2,1,0:T(8,128)(2,1)}), bf16[8,32,128]{2,1,0:T(8,128)(2,1)S(1)}, u32[]{:S(2)}, u32[]{:S(2)}) async-start(bf16[8,32,128]{2,1,0:T(8,128)(2,1)} %bitcast.6), calls=%async_computation | async-start | bytes 131072 | tf_op jit(solution)/shard_map/all_to_all | solution.py:43
  25.7 1.9 copy-start.5
  38.7 3.4 %copy-start.2 = (f32[1280,256]{1,0:T(8,128)S(1)}, f32[1280,256]{1,0:T(8,128)}, u32[]{:S(2)}) copy-start(f32[1280,256]{1,0:T(8,128)} %fusion.34) | copy-start | bytes 3932164
  38.7 3.4 %copy-start.7 = (bf16[1280,256]{1,0:T(8,128)(2,1)S(1)}, bf16[1280,256]{1,0:T(8,128)(2,1)}, u32[]{:S(2)}) copy-start(bf16[1280,256]{1,0:T(8,128)(2,1)} %param.19) | copy-start | bytes 1966084
  38.7 3.4 %copy-start.8 = (bf16[128,256]{1,0:T(8,128)(2,1)S(1)}, bf16[128,256]{1,0:T(8,128)(2,1)}, u32[]{:S(2)}) copy-start(bf16[128,256]{1,0:T(8,128)(2,1)} %param.18) | copy-start | bytes 196612
  50.7 3.6 %copy-start.6 = (s32[48]{0:T(128)S(1)}, s32[48]{0:T(128)}, u32[]{:S(2)}) copy-start(s32[48]{0:T(128)} %param.15) | copy-start | bytes 580
  59.1 8.5 %all-to-all-start.1 = ((bf16[4,32,128]{2,1,0:T(8,128)(2,1)}), bf16[4,32,128]{2,1,0:T(8,128)(2,1)S(1)}, u32[]{:S(2)}, u32[]{:S(2)}) async-start(bf16[4,32,128]{2,1,0:T(8,128)(2,1)} %bitcast.26), calls=%async_computation.1 | async-start | bytes 65536 | tf_op jit(solution)/shard_map/all_to_all | solution.py:94
  62.8 133.5 %all-reduce.3.cloned.1.call-start = ((), (), s32[]{:S(2)}) async-start(), calls=%async_computation.3 | async-start | bytes 524288 | tf_op jit(solution)/shard_map/psum | solution.py:96
  67.5 4.3 %copy-start.4 = (bf16[4,32,128]{2,1,0:T(8,128)(2,1)}, bf16[4,32,128]{2,1,0:T(8,128)(2,1)S(1)}, u32[]{:S(2)}) copy-start(bf16[4,32,128]{2,1,0:T(8,128)(2,1)S(1)} %all-to-all-done.1) | copy-start | bytes 98308
  67.5 10.4 %all-to-all-start.2 = ((bf16[8,32,128]{2,1,0:T(8,128)(2,1)}), bf16[8,32,128]{2,1,0:T(8,128)(2,1)}, u32[]{:S(2)}, u32[]{:S(2)}) async-start(bf16[8,32,128]{2,1,0:T(8,128)(2,1)} %bitcast.21), calls=%async_computation.2 | async-start | bytes 131072 | tf_op jit(solution)/shard_map/all_to_all | solution.py:95
Sparse Core Ops, SparseCore 0:
  69.8 126.3 all-reduce.2
